TPU v7x, 128 devices: a whole 4x4x4 slice. The times are simulated.
128 devices in a mesh: grp: 16 (over y, z), lag: 8 (over x, core).
Axes of the slice: x: 4, y: 4, z: 4, core: 2. Of those that a mesh axis runs over, the one named last changes fastest.
Arguments:
- history: float32 [16, 512, 32, 128], P('lag', 'grp'), may hold values from -6 to 6
- tiles: bfloat16 [65536, 128, 128], P(('grp', 'lag')), may hold values from -0.01171875 to 0.01171875
- tile_src: int32 [65536], P(('grp', 'lag')), may hold values from 0 to 511
- tile_obs: int32 [65536], P(('grp', 'lag')), may hold values from 0 to 32
- tile_lag: int32 [65536], P(('grp', 'lag')), may hold values from 0 to 1
- incident: float32 [32, 32, 128], P('grp', 'lag'), may hold values from -6 to 6
- near_inverse: bfloat16 [32, 128, 128], P('grp'), may hold values from -0.5 to 0.5
Outputs:
- field: float32 [32, 32, 128], P('grp', 'lag')
- new_current: float32 [32, 32, 128], P('grp', 'lag')
Inputs may be any that keep to these rules, and one draw needn't show every extreme that they name: `tile_obs`: a value of 32 marks a padded tile.
All inputs are finite; a program needn't handle non-finite values.
Results may differ from a plain program's by a relative error of at most 0.0035.
Values may be sent and summed in bfloat16 or wider, within the bound.
No kernel may reach another device: no remote copies, remote signals or barrier semaphores. Data moves between devices by JAX's collectives and lax.ppermute only.
A program may use at most 128 MiB of HBM per device.

v0:
```python
import jax
import jax.numpy as jnp
from jax import lax
from jax.sharding import PartitionSpec as P

OBS_DEV = 2


def body(history, tiles, tile_src, tile_obs, tile_lag, incident, near_inverse):
    hist16 = history.astype(jnp.bfloat16)
    gathered = lax.all_gather(hist16, "grp", axis=1, tiled=True)
    lag_count = gathered.shape[0]
    source_count = gathered.shape[1]
    flat = gathered.reshape(lag_count * source_count, gathered.shape[2], gathered.shape[3])
    picked = flat[tile_lag * source_count + tile_src]
    terms = jnp.einsum("kas,kos->kao", picked, tiles, preferred_element_type=jnp.float32)
    observers = OBS_DEV * lax.axis_size("grp")
    partial_field = jax.ops.segment_sum(terms, tile_obs, num_segments=observers)
    angle_part = incident.shape[1]
    summed = lax.psum(partial_field, "lag")
    mine = lax.psum_scatter(summed, "grp", scatter_dimension=0, tiled=True)
    field = lax.dynamic_slice_in_dim(mine, lax.axis_index("lag") * angle_part, angle_part, 1)
    rhs = (incident - field).astype(jnp.bfloat16)
    new_current = jnp.einsum("oag,ohg->oah", rhs, near_inverse, preferred_element_type=jnp.float32)
    return (field, new_current)


def solution(mesh):
    return jax.shard_map(
        body,
        mesh=mesh,
        in_specs=(
            P("lag", "grp", None, None),
            P(("grp", "lag"), None, None),
            P(("grp", "lag")),
            P(("grp", "lag")),
            P(("grp", "lag")),
            P("grp", "lag", None),
            P("grp", None, None),
        ),
        out_specs=(P("grp", "lag", None), P("grp", "lag", None)),
        check_vma=False,
    )
```

profile of v0, /device:TPU:0, one launch (start us, length us, event | category | flops | bytes accessed | tf_op | source)
XLA Modules:
  0.0 255.2 jit_solution(2422170448194656881)
XLA Ops:
  7.2 0.0 copy-start
  7.2 0.0 all-gather.2.cloned.1.call-start
  7.2 2.2 convert_element_type.6
  9.4 0.0 all-gather.2.cloned.1.call-update
  9.4 0.0 reduce-scatter.2.cloned.1.call-start
  9.5 0.7 compare_select_fusion
  10.2 73.4 %all-gather.2.cloned.1.call-done = bf16[2,512,32,128]{3,2,1,0:T(8,128)(2,1)} async-done(((bf16[2,32,32,128]{3,2,1,0:T(8,128)(2,1)}), bf16[2,512,32,128]{3,2,1,0:T(8,128)(2,1)}) %all-gather.2.cloned.1.call-update) | async-done | bytes 8388624 | tf_op jit(solution)/shard_map/all_gather | solution.py:11
  83.6 6.5 %gather_fusion = bf16[512,32,128]{2,1,0:T(8,128)(2,1)} fusion(bf16[1024,32,128]{2,1,0:T(8,128)(2,1)} %bitcast.4, s32[1024]{0:T(1024)S(1)} %pad_clamp_fusion), kind=kCustom, calls=%fused_computation | custom fusion | bytes 8390656 | tf_op jit(solution)/shard_map/gather | solution.py:15
  90.1 0.0 copy-start.4
  90.1 15.0 %fusion.1 = f32[512,32,128]{2,1,0:T(8,128)} fusion(bf16[512,32,128]{2,1,0:T(8,128)(2,1)} %gather_fusion, bf16[512,128,128]{2,1,0:T(8,128)(2,1)} %param.8), kind=kOutput, calls=%fused_computation.7 | convolution fusion | flops 536870912 | bytes 29360128 | tf_op jit(solution)/shard_map/kas,kos->kao/dot_general | solution.py:16
  105.2 0.0 copy-done.4
  105.2 0.0 copy-start.3
  105.2 44.7 %scatter_fusion = f32[32,32,128]{2,1,0:T(8,128)S(1)} fusion(f32[32,32,128]{2,1,0:T(8,128)S(1)} %broadcast_in_dim.9, s32[512]{0:T(512)S(1)} %copy-done.4, f32[512,32,128]{2,1,0:T(8,128)} %fusion.1), kind=kCustom, calls=%fused_computation.1 | custom fusion | flops 2097152 | bytes 25167872 | tf_op jit(solution)/shard_map/scatter-add | solution.py:18
  149.9 0.0 copy-start.1
  149.9 0.8 copy-done.1
  150.7 0.0 reduce-scatter.2.cloned.1.call-update
  150.7 72.3 %reduce-scatter.2.cloned.1.call-done = f32[2,32,128]{2,1,0:T(8,128)} async-done(((f32[32,32,128]{2,1,0:T(8,128)}), f32[2,32,128]{2,1,0:T(8,128)}) %reduce-scatter.2.cloned.1.call-update) | async-done | bytes 32784 | tf_op jit(solution)/shard_map/reduce_scatter | solution.py:21
  223.0 24.6 %psum.8 = f32[2,32,128]{2,1,0:T(8,128)S(1)} all-reduce(f32[2,32,128]{2,1,0:T(8,128)} %reduce-scatter.2.cloned.1.call-done), channel_id=1, replica_groups=mesh['grp'=16,'lag'=8] {'lag'}, use_global_device_ids=true, to_apply=%region_1.0 | all-reduce | flops 8192 | bytes 65536 | tf_op jit(solution)/shard_map/psum | solution.py:20
  247.6 0.0 copy-done
  247.6 0.0 copy-done.3
  247.6 0.0 copy-start.2
  247.6 0.7 fusion
  248.4 0.0 copy-done.2
  (3 shorter events, 0.1 us)
Async XLA Ops:
  7.2 240.4 %copy-start = (bf16[2,128,128]{2,1,0:T(8,128)(2,1)S(1)}, bf16[2,128,128]{2,1,0:T(8,128)(2,1)}, u32[]{:S(2)}) copy-start(bf16[2,128,128]{2,1,0:T(8,128)(2,1)} %param.13) | copy-start | bytes 196612
  7.2 76.4 %all-gather.2.cloned.1.call-start = ((), (), s32[]{:S(2)}) async-start(), calls=%async_computation.1 | async-start | bytes 8912896 | tf_op jit(solution)/shard_map/all_gather | solution.py:11
  9.4 213.6 %reduce-scatter.2.cloned.1.call-start = ((), (), s32[]{:S(2)}) async-start(), calls=%async_computation.2 | async-start | bytes 557056 | tf_op jit(solution)/shard_map/reduce_scatter | solution.py:21
  90.1 15.0 %copy-start.4 = (s32[512]{0:T(512)S(1)}, s32[512]{0:T(512)}, u32[]{:S(2)}) copy-start(s32[512]{0:T(512)} %param.10) | copy-start | bytes 6148
  105.2 142.4 %copy-start.3 = (f32[2,4,128]{2,1,0:T(4,128)S(1)}, f32[2,4,128]{2,1,0:T(4,128)}, u32[]{:S(2)}) copy-start(f32[2,4,128]{2,1,0:T(4,128)} %param.12) | copy-start | bytes 12292
  149.9 0.8 copy-start.1
  247.6 0.8 copy-start.2
Sparse Core Ops, SparseCore 0:
  10.2 73.3 all-gather.1
  150.8 72.1 reduce-scatter.1
where the time goes:
time: 256 us; the launch traced here: 255 us
  waiting for transfers between devices  146 us (57%)
  other arithmetic  47.6 us (19%)
  blocking collectives  24.6 us (10%)
  matrix products  15.7 us (6%)
  between operations  14.1 us (6%)
  local copies, waits for them, and re-layouts  7.41 us (3%)
    all_gather x1, waiting for transfers between devices, body(): gathered = lax.all_gather(hist16, 'grp', axis=1, tiled=True)  73.4 us
    reduce_scatter x1, waiting for transfers between devices, body(): mine = lax.psum_scatter(summed, 'grp', scatter_dimension=0, tiled=True)  72.3 us
    scatter-add x1, other arithmetic, body(): partial_field = jax.ops.segment_sum(terms, tile_obs, num_segments=observers)  44.7 us
    psum x1, blocking collectives, body(): summed = lax.psum(partial_field, 'lag')  24.6 us
    dot_general x1, matrix products, body(): jnp.einsum('kas,kos->kao', picked, tiles, preferred_element_type=jnp.floa...  15 us
    gather x1, local copies, waits for them, and re-layouts, body(): picked = flat[tile_lag * source_count + tile_src]  6.55 us
  transfers between devices with their start and end apart: 2, of which 2 were waited for; matrix products, arithmetic and copies ran while one was open for 0% of the time, Pallas kernels for 0%

commit v1 on v0

--- a/solution.py
+++ b/solution.py
@@ -6,9 +6,19 @@
 OBS_DEV = 2
 
 
+def around_the_ring(block, axis, dim):
+    size = lax.axis_size(axis)
+    held, blocks = (block, [block])
+    for _ in range(size - 1):
+        held = lax.ppermute(held, axis, [(i, (i + 1) % size) for i in range(size)])
+        blocks.insert(0, held)
+    line = jnp.concatenate(blocks, axis=dim)
+    return jnp.roll(line, (lax.axis_index(axis) + 1) * block.shape[dim], axis=dim)
+
+
 def body(history, tiles, tile_src, tile_obs, tile_lag, incident, near_inverse):
     hist16 = history.astype(jnp.bfloat16)
-    gathered = lax.all_gather(hist16, "grp", axis=1, tiled=True)
+    gathered = around_the_ring(hist16, "grp", 1)
     lag_count = gathered.shape[0]
     source_count = gathered.shape[1]
     flat = gathered.reshape(lag_count * source_count, gathered.shape[2], gathered.shape[3])

time: 256 us -> 464 us (1.81)
  waiting for transfers between devices: 146 us -> 294 us
  local copies, waits for them, and re-layouts: 7.41 us -> 62.8 us
    ppermute x0 -> x15, waiting for transfers between devices: none -> 225 us  [around_the_ring(): held = lax.ppermute(held, axis, [(i, (i + 1) % size) for i in range(size)])]
    all_gather x1 -> x0, waiting for transfers between devices: 73.4 us -> none  [body(): gathered = lax.all_gather(hist16, 'grp', axis=1, tiled=True)]
    unnamed x10 -> x78, local copies, waits for them, and re-layouts: 0.81 us -> 48.1 us
    dynamic_slice x0 -> x1, local copies, waits for them, and re-layouts: none -> 8.1 us  [around_the_ring(): jnp.roll(line, (lax.axis_index(axis) + 1) * block.shape[dim], axis=dim)]
  transfers between devices with their start and end apart: 2 -> 16, of which waited for: 2 -> 16; matrix products, arithmetic and copies ran while one was open for 0% -> 0% of each run, Pallas kernels for 0% -> 0%
where the time goes in v1:
time: 464 us; the launch traced here: 462 us
  waiting for transfers between devices  294 us (63%)
  local copies, waits for them, and re-layouts  62.8 us (14%)
  other arithmetic  48.7 us (10%)
  blocking collectives  24.6 us (5%)
  matrix products  15.8 us (3%)
  between operations  14.2 us (3%)
    ppermute x15, waiting for transfers between devices, around_the_ring(): held = lax.ppermute(held, axis, [(i, (i + 1) % size) for i in range(size)])  225 us
    reduce_scatter x1, waiting for transfers between devices, body(): mine = lax.psum_scatter(summed, 'grp', scatter_dimension=0, tiled=True)  68.9 us
    unnamed x78, local copies, waits for them, and re-layouts  48.1 us
    scatter-add x1, other arithmetic, body(): partial_field = jax.ops.segment_sum(terms, tile_obs, num_segments=observers)  44.7 us
    psum x1, blocking collectives, body(): summed = lax.psum(partial_field, 'lag')  24.6 us
    dot_general x1, matrix products, body(): jnp.einsum('kas,kos->kao', picked, tiles, preferred_element_type=jnp.floa...  15 us
  transfers between devices with their start and end apart: 16, of which 16 were waited for; matrix products, arithmetic and copies ran while one was open for 0% of the time, Pallas kernels for 0%

profile of v1, /device:TPU:0, one launch (start us, length us, event | category | flops | bytes accessed | tf_op | source)
XLA Modules:
  0.0 461.9 jit_solution(14060553345037501640)
XLA Ops:
  8.6 2.1 collective-permute-start
  10.7 16.5 %collective-permute-done = bf16[2,32,32,128]{3,2,1,0:T(8,128)(2,1)S(1)} collective-permute-done((bf16[2,32,32,128]{3,2,1,0:T(8,128)(2,1)S(1)}, bf16[2,32,32,128]{3,2,1,0:T(8,128)(2,1)S(1)}, u32[]{:S(2)}, u32[]{:S(2)}) %collective-permute-start) | collective-permute-done | bytes 524320 | tf_op jit(solution)/shard_map/ppermute | solution.py:13
  27.2 16.4 %collective-permute-done.1 = bf16[2,32,32,128]{3,2,1,0:T(8,128)(2,1)S(1)} collective-permute-done((bf16[2,32,32,128]{3,2,1,0:T(8,128)(2,1)S(1)}, bf16[2,32,32,128]{3,2,1,0:T(8,128)(2,1)S(1)}, u32[]{:S(2)}, u32[]{:S(2)}) %collective-permute-start.1) | collective-permute-done | bytes 524320 | tf_op jit(solution)/shard_map/ppermute | solution.py:13
  43.6 15.5 %collective-permute-done.2 = bf16[2,32,32,128]{3,2,1,0:T(8,128)(2,1)S(1)} collective-permute-done((bf16[2,32,32,128]{3,2,1,0:T(8,128)(2,1)S(1)}, bf16[2,32,32,128]{3,2,1,0:T(8,128)(2,1)S(1)}, u32[]{:S(2)}, u32[]{:S(2)}) %collective-permute-start.2) | collective-permute-done | bytes 524320 | tf_op jit(solution)/shard_map/ppermute | solution.py:13
  59.1 14.6 %collective-permute-done.3 = bf16[2,32,32,128]{3,2,1,0:T(8,128)(2,1)S(1)} collective-permute-done((bf16[2,32,32,128]{3,2,1,0:T(8,128)(2,1)S(1)}, bf16[2,32,32,128]{3,2,1,0:T(8,128)(2,1)S(1)}, u32[]{:S(2)}, u32[]{:S(2)}) %collective-permute-start.3) | collective-permute-done | bytes 524320 | tf_op jit(solution)/shard_map/ppermute | solution.py:13
  73.7 13.7 %collective-permute-done.4 = bf16[2,32,32,128]{3,2,1,0:T(8,128)(2,1)S(1)} collective-permute-done((bf16[2,32,32,128]{3,2,1,0:T(8,128)(2,1)S(1)}, bf16[2,32,32,128]{3,2,1,0:T(8,128)(2,1)S(1)}, u32[]{:S(2)}, u32[]{:S(2)}) %collective-permute-start.4) | collective-permute-done | bytes 524320 | tf_op jit(solution)/shard_map/ppermute | solution.py:13
  88.2 12.7 %collective-permute-done.5 = bf16[2,32,32,128]{3,2,1,0:T(8,128)(2,1)S(1)} collective-permute-done((bf16[2,32,32,128]{3,2,1,0:T(8,128)(2,1)S(1)}, bf16[2,32,32,128]{3,2,1,0:T(8,128)(2,1)S(1)}, u32[]{:S(2)}, u32[]{:S(2)}) %collective-permute-start.5) | collective-permute-done | bytes 524320 | tf_op jit(solution)/shard_map/ppermute | solution.py:13
  101.7 12.5 %collective-permute-done.6 = bf16[2,32,32,128]{3,2,1,0:T(8,128)(2,1)S(1)} collective-permute-done((bf16[2,32,32,128]{3,2,1,0:T(8,128)(2,1)S(1)}, bf16[2,32,32,128]{3,2,1,0:T(8,128)(2,1)S(1)}, u32[]{:S(2)}, u32[]{:S(2)}) %collective-permute-start.6) | collective-permute-done | bytes 524320 | tf_op jit(solution)/shard_map/ppermute | solution.py:13
  115.1 13.3 %collective-permute-done.7 = bf16[2,32,32,128]{3,2,1,0:T(8,128)(2,1)S(1)} collective-permute-done((bf16[2,32,32,128]{3,2,1,0:T(8,128)(2,1)S(1)}, bf16[2,32,32,128]{3,2,1,0:T(8,128)(2,1)S(1)}, u32[]{:S(2)}, u32[]{:S(2)}) %collective-permute-start.7) | collective-permute-done | bytes 524320 | tf_op jit(solution)/shard_map/ppermute | solution.py:13
  129.2 14.4 %collective-permute-done.8 = bf16[2,32,32,128]{3,2,1,0:T(8,128)(2,1)S(1)} collective-permute-done((bf16[2,32,32,128]{3,2,1,0:T(8,128)(2,1)S(1)}, bf16[2,32,32,128]{3,2,1,0:T(8,128)(2,1)S(1)}, u32[]{:S(2)}, u32[]{:S(2)}) %collective-permute-start.8) | collective-permute-done | bytes 524320 | tf_op jit(solution)/shard_map/ppermute | solution.py:13
  144.4 15.5 %collective-permute-done.9 = bf16[2,32,32,128]{3,2,1,0:T(8,128)(2,1)S(1)} collective-permute-done((bf16[2,32,32,128]{3,2,1,0:T(8,128)(2,1)S(1)}, bf16[2,32,32,128]{3,2,1,0:T(8,128)(2,1)S(1)}, u32[]{:S(2)}, u32[]{:S(2)}) %collective-permute-start.9) | collective-permute-done | bytes 524320 | tf_op jit(solution)/shard_map/ppermute | solution.py:13
  160.7 16.6 %collective-permute-done.10 = bf16[2,32,32,128]{3,2,1,0:T(8,128)(2,1)S(1)} collective-permute-done((bf16[2,32,32,128]{3,2,1,0:T(8,128)(2,1)S(1)}, bf16[2,32,32,128]{3,2,1,0:T(8,128)(2,1)S(1)}, u32[]{:S(2)}, u32[]{:S(2)}) %collective-permute-start.10) | collective-permute-done | bytes 524320 | tf_op jit(solution)/shard_map/ppermute | solution.py:13
  178.1 17.8 %collective-permute-done.11 = bf16[2,32,32,128]{3,2,1,0:T(8,128)(2,1)S(1)} collective-permute-done((bf16[2,32,32,128]{3,2,1,0:T(8,128)(2,1)S(1)}, bf16[2,32,32,128]{3,2,1,0:T(8,128)(2,1)S(1)}, u32[]{:S(2)}, u32[]{:S(2)}) %collective-permute-start.11) | collective-permute-done | bytes 524320 | tf_op jit(solution)/shard_map/ppermute | solution.py:13
  196.7 17.3 %collective-permute-done.12 = bf16[2,32,32,128]{3,2,1,0:T(8,128)(2,1)S(1)} collective-permute-done((bf16[2,32,32,128]{3,2,1,0:T(8,128)(2,1)S(1)}, bf16[2,32,32,128]{3,2,1,0:T(8,128)(2,1)S(1)}, u32[]{:S(2)}, u32[]{:S(2)}) %collective-permute-start.12) | collective-permute-done | bytes 524320 | tf_op jit(solution)/shard_map/ppermute | solution.py:13
  214.8 16.0 %collective-permute-done.13 = bf16[2,32,32,128]{3,2,1,0:T(8,128)(2,1)} collective-permute-done((bf16[2,32,32,128]{3,2,1,0:T(8,128)(2,1)S(1)}, bf16[2,32,32,128]{3,2,1,0:T(8,128)(2,1)}, u32[]{:S(2)}, u32[]{:S(2)}) %collective-permute-start.13) | collective-permute-done | bytes 524320 | tf_op jit(solution)/shard_map/ppermute | solution.py:13
  231.7 11.9 %collective-permute-done.14 = bf16[2,32,32,128]{3,2,1,0:T(8,128)(2,1)} collective-permute-done((bf16[2,32,32,128]{3,2,1,0:T(8,128)(2,1)}, bf16[2,32,32,128]{3,2,1,0:T(8,128)(2,1)}, u32[]{:S(2)}, u32[]{:S(2)}) %collective-permute-start.14) | collective-permute-done | bytes 524320 | tf_op jit(solution)/shard_map/ppermute | solution.py:13
  243.6 1.9 constant_dynamic-update-slice_fusion.31
  245.5 1.9 constant_dynamic-update-slice_fusion.30
  249.4 1.9 constant_dynamic-update-slice_fusion.28
  251.3 1.9 constant_dynamic-update-slice_fusion.27
  255.2 1.9 constant_dynamic-update-slice_fusion.25
  257.1 1.9 constant_dynamic-update-slice_fusion.24
  259.0 1.9 constant_dynamic-update-slice_fusion.23
  262.9 1.9 constant_dynamic-update-slice_fusion.21
  269.2 1.9 constant_dynamic-update-slice_fusion.15
  271.1 1.9 constant_dynamic-update-slice_fusion.14
  285.5 8.1 %constant_dynamic-slice_fusion.1 = bf16[2,512,32,128]{3,2,1,0:T(8,128)(2,1)} fusion(bf16[2,1024,32,128]{3,2,1,0:T(8,128)(2,1)} %constant_dynamic-update-slice_fusion, s32[]{:T(128)S(6)} %select_n.20), kind=kLoop, calls=%fused_computation.39 | loop fusion | bytes 16777220 | tf_op jit(solution)/shard_map/jit(_roll_dynamic)/dynamic_slice | solution.py:16
  293.5 6.6 %gather_fusion = bf16[512,32,128]{2,1,0:T(8,128)(2,1)} fusion(bf16[1024,32,128]{2,1,0:T(8,128)(2,1)} %bitcast.4, s32[1024]{0:T(1024)S(1)} %pad_clamp_fusion), kind=kCustom, calls=%fused_computation | custom fusion | bytes 8390656 | tf_op jit(solution)/shard_map/gather | solution.py:25
  300.1 15.0 %fusion.1 = f32[512,32,128]{2,1,0:T(8,128)} fusion(bf16[512,32,128]{2,1,0:T(8,128)(2,1)} %gather_fusion, bf16[512,128,128]{2,1,0:T(8,128)(2,1)} %param.8), kind=kOutput, calls=%fused_computation.40 | convolution fusion | flops 536870912 | bytes 29360128 | tf_op jit(solution)/shard_map/kas,kos->kao/dot_general | solution.py:26
  315.2 44.7 %scatter_fusion = f32[32,32,128]{2,1,0:T(8,128)S(1)} fusion(f32[32,32,128]{2,1,0:T(8,128)S(1)} %broadcast_in_dim.9, s32[512]{0:T(512)S(1)} %copy-done.23, f32[512,32,128]{2,1,0:T(8,128)} %fusion.1), kind=kCustom, calls=%fused_computation.1 | custom fusion | flops 2097152 | bytes 25167872 | tf_op jit(solution)/shard_map/scatter-add | solution.py:28
  360.7 68.9 %reduce-scatter.2.cloned.1.call-done = f32[2,32,128]{2,1,0:T(8,128)} async-done(((f32[32,32,128]{2,1,0:T(8,128)}), f32[2,32,128]{2,1,0:T(8,128)}) %reduce-scatter.2.cloned.1.call-update) | async-done | bytes 32784 | tf_op jit(solution)/shard_map/reduce_scatter | solution.py:31
  429.6 24.6 %psum.8 = f32[2,32,128]{2,1,0:T(8,128)S(1)} all-reduce(f32[2,32,128]{2,1,0:T(8,128)} %reduce-scatter.2.cloned.1.call-done), channel_id=1, replica_groups=mesh['grp'=16,'lag'=8] {'lag'}, use_global_device_ids=true, to_apply=%region_1.2 | all-reduce | flops 8192 | bytes 65536 | tf_op jit(solution)/shard_map/psum | solution.py:30
  (92 shorter events, 33.7 us)
Async XLA Ops:
  7.2 447.1 %copy-start = (bf16[2,128,128]{2,1,0:T(8,128)(2,1)S(1)}, bf16[2,128,128]{2,1,0:T(8,128)(2,1)}, u32[]{:S(2)}) copy-start(bf16[2,128,128]{2,1,0:T(8,128)(2,1)} %param.13) | copy-start | bytes 196612
  7.2 261.1 %copy-start.2 = (f32[2,32,32,128]{3,2,1,0:T(8,128)S(1)}, f32[2,32,32,128]{3,2,1,0:T(8,128)}, u32[]{:S(2)}) copy-start(f32[2,32,32,128]{3,2,1,0:T(8,128)} %param.7) | copy-start | bytes 3145732
  7.2 422.4 %reduce-scatter.2.cloned.1.call-start = ((), (), s32[]{:S(2)}) async-start(), calls=%async_computation.1 | async-start | bytes 557056 | tf_op jit(solution)/shard_map/reduce_scatter | solution.py:31
  8.6 18.6 %collective-permute-start = (bf16[2,32,32,128]{3,2,1,0:T(8,128)(2,1)S(1)}, bf16[2,32,32,128]{3,2,1,0:T(8,128)(2,1)S(1)}, u32[]{:S(2)}, u32[]{:S(2)}) collective-permute-start(bf16[2,32,32,128]{3,2,1,0:T(8,128)(2,1)S(1)} %convert_element_type.6), channel_id=1, source_target_pairs={{0,8},{8,16},{16,24},{24,32},{32,40},{40,48},{48,56},{56,64},{64,7... | collective-permute-start | bytes 1572872 | tf_op jit(solution)/shard_map/ppermute | solution.py:13
  27.2 16.4 %collective-permute-start.1 = (bf16[2,32,32,128]{3,2,1,0:T(8,128)(2,1)S(1)}, bf16[2,32,32,128]{3,2,1,0:T(8,128)(2,1)S(1)}, u32[]{:S(2)}, u32[]{:S(2)}) collective-permute-start(bf16[2,32,32,128]{3,2,1,0:T(8,128)(2,1)S(1)} %collective-permute-done), channel_id=1, source_target_pairs={{0,8},{8,16},{16,24},{24,32},{32,40},{40,48},{48,56},{56,64},{64,7... | collective-permute-start | bytes 1572872 | tf_op jit(solution)/shard_map/ppermute | solution.py:13
  43.6 15.5 %collective-permute-start.2 = (bf16[2,32,32,128]{3,2,1,0:T(8,128)(2,1)S(1)}, bf16[2,32,32,128]{3,2,1,0:T(8,128)(2,1)S(1)}, u32[]{:S(2)}, u32[]{:S(2)}) collective-permute-start(bf16[2,32,32,128]{3,2,1,0:T(8,128)(2,1)S(1)} %collective-permute-done.1), channel_id=1, source_target_pairs={{0,8},{8,16},{16,24},{24,32},{32,40},{40,48},{48,56},{56,64},{64,7... | collective-permute-start | bytes 1572872 | tf_op jit(solution)/shard_map/ppermute | solution.py:13
  59.1 14.6 %collective-permute-start.3 = (bf16[2,32,32,128]{3,2,1,0:T(8,128)(2,1)S(1)}, bf16[2,32,32,128]{3,2,1,0:T(8,128)(2,1)S(1)}, u32[]{:S(2)}, u32[]{:S(2)}) collective-permute-start(bf16[2,32,32,128]{3,2,1,0:T(8,128)(2,1)S(1)} %collective-permute-done.2), channel_id=1, source_target_pairs={{0,8},{8,16},{16,24},{24,32},{32,40},{40,48},{48,56},{56,64},{64,7... | collective-permute-start | bytes 1572872 | tf_op jit(solution)/shard_map/ppermute | solution.py:13
  73.7 13.7 %collective-permute-start.4 = (bf16[2,32,32,128]{3,2,1,0:T(8,128)(2,1)S(1)}, bf16[2,32,32,128]{3,2,1,0:T(8,128)(2,1)S(1)}, u32[]{:S(2)}, u32[]{:S(2)}) collective-permute-start(bf16[2,32,32,128]{3,2,1,0:T(8,128)(2,1)S(1)} %collective-permute-done.3), channel_id=1, source_target_pairs={{0,8},{8,16},{16,24},{24,32},{32,40},{40,48},{48,56},{56,64},{64,7... | collective-permute-start | bytes 1572872 | tf_op jit(solution)/shard_map/ppermute | solution.py:13
  88.2 12.7 %collective-permute-start.5 = (bf16[2,32,32,128]{3,2,1,0:T(8,128)(2,1)S(1)}, bf16[2,32,32,128]{3,2,1,0:T(8,128)(2,1)S(1)}, u32[]{:S(2)}, u32[]{:S(2)}) collective-permute-start(bf16[2,32,32,128]{3,2,1,0:T(8,128)(2,1)S(1)} %collective-permute-done.4), channel_id=1, source_target_pairs={{0,8},{8,16},{16,24},{24,32},{32,40},{40,48},{48,56},{56,64},{64,7... | collective-permute-start | bytes 1572872 | tf_op jit(solution)/shard_map/ppermute | solution.py:13
  101.7 12.5 %collective-permute-start.6 = (bf16[2,32,32,128]{3,2,1,0:T(8,128)(2,1)S(1)}, bf16[2,32,32,128]{3,2,1,0:T(8,128)(2,1)S(1)}, u32[]{:S(2)}, u32[]{:S(2)}) collective-permute-start(bf16[2,32,32,128]{3,2,1,0:T(8,128)(2,1)S(1)} %collective-permute-done.5), channel_id=1, source_target_pairs={{0,8},{8,16},{16,24},{24,32},{32,40},{40,48},{48,56},{56,64},{64,7... | collective-permute-start | bytes 1572872 | tf_op jit(solution)/shard_map/ppermute | solution.py:13
  114.2 0.8 copy-start.7
  115.0 13.4 %collective-permute-start.7 = (bf16[2,32,32,128]{3,2,1,0:T(8,128)(2,1)S(1)}, bf16[2,32,32,128]{3,2,1,0:T(8,128)(2,1)S(1)}, u32[]{:S(2)}, u32[]{:S(2)}) collective-permute-start(bf16[2,32,32,128]{3,2,1,0:T(8,128)(2,1)S(1)} %collective-permute-done.6), channel_id=1, source_target_pairs={{0,8},{8,16},{16,24},{24,32},{32,40},{40,48},{48,56},{56,64},{64,7... | collective-permute-start | bytes 1572872 | tf_op jit(solution)/shard_map/ppermute | solution.py:13
  129.2 14.4 %collective-permute-start.8 = (bf16[2,32,32,128]{3,2,1,0:T(8,128)(2,1)S(1)}, bf16[2,32,32,128]{3,2,1,0:T(8,128)(2,1)S(1)}, u32[]{:S(2)}, u32[]{:S(2)}) collective-permute-start(bf16[2,32,32,128]{3,2,1,0:T(8,128)(2,1)S(1)} %collective-permute-done.7), channel_id=1, source_target_pairs={{0,8},{8,16},{16,24},{24,32},{32,40},{40,48},{48,56},{56,64},{64,7... | collective-permute-start | bytes 1572872 | tf_op jit(solution)/shard_map/ppermute | solution.py:13
  143.6 0.8 copy-start.11
  144.4 15.5 %collective-permute-start.9 = (bf16[2,32,32,128]{3,2,1,0:T(8,128)(2,1)S(1)}, bf16[2,32,32,128]{3,2,1,0:T(8,128)(2,1)S(1)}, u32[]{:S(2)}, u32[]{:S(2)}) collective-permute-start(bf16[2,32,32,128]{3,2,1,0:T(8,128)(2,1)S(1)} %collective-permute-done.8), channel_id=1, source_target_pairs={{0,8},{8,16},{16,24},{24,32},{32,40},{40,48},{48,56},{56,64},{64,7... | collective-permute-start | bytes 1572872 | tf_op jit(solution)/shard_map/ppermute | solution.py:13
  160.7 16.6 %collective-permute-start.10 = (bf16[2,32,32,128]{3,2,1,0:T(8,128)(2,1)S(1)}, bf16[2,32,32,128]{3,2,1,0:T(8,128)(2,1)S(1)}, u32[]{:S(2)}, u32[]{:S(2)}) collective-permute-start(bf16[2,32,32,128]{3,2,1,0:T(8,128)(2,1)S(1)} %collective-permute-done.9), channel_id=1, source_target_pairs={{0,8},{8,16},{16,24},{24,32},{32,40},{40,48},{48,56},{56,64},{64,7... | collective-permute-start | bytes 1572872 | tf_op jit(solution)/shard_map/ppermute | solution.py:13
  178.1 17.8 %collective-permute-start.11 = (bf16[2,32,32,128]{3,2,1,0:T(8,128)(2,1)S(1)}, bf16[2,32,32,128]{3,2,1,0:T(8,128)(2,1)S(1)}, u32[]{:S(2)}, u32[]{:S(2)}) collective-permute-start(bf16[2,32,32,128]{3,2,1,0:T(8,128)(2,1)S(1)} %collective-permute-done.10), channel_id=1, source_target_pairs={{0,8},{8,16},{16,24},{24,32},{32,40},{40,48},{48,56},{56,64},{64,7... | collective-permute-start | bytes 1572872 | tf_op jit(solution)/shard_map/ppermute | solution.py:13
  196.7 17.3 %collective-permute-start.12 = (bf16[2,32,32,128]{3,2,1,0:T(8,128)(2,1)S(1)}, bf16[2,32,32,128]{3,2,1,0:T(8,128)(2,1)S(1)}, u32[]{:S(2)}, u32[]{:S(2)}) collective-permute-start(bf16[2,32,32,128]{3,2,1,0:T(8,128)(2,1)S(1)} %collective-permute-done.11), channel_id=1, source_target_pairs={{0,8},{8,16},{16,24},{24,32},{32,40},{40,48},{48,56},{56,64},{64,7... | collective-permute-start | bytes 1572872 | tf_op jit(solution)/shard_map/ppermute | solution.py:13
  214.0 0.8 copy-start.19
  214.8 16.0 %collective-permute-start.13 = (bf16[2,32,32,128]{3,2,1,0:T(8,128)(2,1)S(1)}, bf16[2,32,32,128]{3,2,1,0:T(8,128)(2,1)}, u32[]{:S(2)}, u32[]{:S(2)}) collective-permute-start(bf16[2,32,32,128]{3,2,1,0:T(8,128)(2,1)S(1)} %collective-permute-done.12), channel_id=1, source_target_pairs={{0,8},{8,16},{16,24},{24,32},{32,40},{40,48},{48,56},{56,64},{64,7... | collective-permute-start | bytes 1572872 | tf_op jit(solution)/shard_map/ppermute | solution.py:13
  230.8 12.8 %collective-permute-start.14 = (bf16[2,32,32,128]{3,2,1,0:T(8,128)(2,1)}, bf16[2,32,32,128]{3,2,1,0:T(8,128)(2,1)}, u32[]{:S(2)}, u32[]{:S(2)}) collective-permute-start(bf16[2,32,32,128]{3,2,1,0:T(8,128)(2,1)} %collective-permute-done.13), channel_id=1, source_target_pairs={{0,8},{8,16},{16,24},{24,32},{32,40},{40,48},{48,56},{56,64},{64,7... | collective-permute-start | bytes 1572872 | tf_op jit(solution)/shard_map/ppermute | solution.py:13
  230.8 42.3 %copy-start.20 = (bf16[2,32,32,128]{3,2,1,0:T(8,128)(2,1)S(1)}, bf16[2,32,32,128]{3,2,1,0:T(8,128)(2,1)}, u32[]{:S(2)}) copy-start(bf16[2,32,32,128]{3,2,1,0:T(8,128)(2,1)} %copy-done.19) | copy-start | bytes 1572868
  230.8 43.1 %copy-start.18 = (bf16[2,32,32,128]{3,2,1,0:T(8,128)(2,1)S(1)}, bf16[2,32,32,128]{3,2,1,0:T(8,128)(2,1)}, u32[]{:S(2)}) copy-start(bf16[2,32,32,128]{3,2,1,0:T(8,128)(2,1)} %copy-done.17) | copy-start | bytes 1572868
  230.8 44.0 %copy-start.16 = (bf16[2,32,32,128]{3,2,1,0:T(8,128)(2,1)S(1)}, bf16[2,32,32,128]{3,2,1,0:T(8,128)(2,1)}, u32[]{:S(2)}) copy-start(bf16[2,32,32,128]{3,2,1,0:T(8,128)(2,1)} %copy-done.15) | copy-start | bytes 1572868
  230.8 44.9 %copy-start.14 = (bf16[2,32,32,128]{3,2,1,0:T(8,128)(2,1)S(1)}, bf16[2,32,32,128]{3,2,1,0:T(8,128)(2,1)}, u32[]{:S(2)}) copy-start(bf16[2,32,32,128]{3,2,1,0:T(8,128)(2,1)} %copy-done.13) | copy-start | bytes 1572868
  230.8 45.8 %copy-start.12 = (bf16[2,32,32,128]{3,2,1,0:T(8,128)(2,1)S(1)}, bf16[2,32,32,128]{3,2,1,0:T(8,128)(2,1)}, u32[]{:S(2)}) copy-start(bf16[2,32,32,128]{3,2,1,0:T(8,128)(2,1)} %copy-done.11) | copy-start | bytes 1572868
  230.8 46.6 %copy-start.10 = (bf16[2,32,32,128]{3,2,1,0:T(8,128)(2,1)S(1)}, bf16[2,32,32,128]{3,2,1,0:T(8,128)(2,1)}, u32[]{:S(2)}) copy-start(bf16[2,32,32,128]{3,2,1,0:T(8,128)(2,1)} %copy-done.9) | copy-start | bytes 1572868
  230.8 47.5 %copy-start.8 = (bf16[2,32,32,128]{3,2,1,0:T(8,128)(2,1)S(1)}, bf16[2,32,32,128]{3,2,1,0:T(8,128)(2,1)}, u32[]{:S(2)}) copy-start(bf16[2,32,32,128]{3,2,1,0:T(8,128)(2,1)} %copy-done.7) | copy-start | bytes 1572868
  230.8 48.4 %copy-start.6 = (bf16[2,32,32,128]{3,2,1,0:T(8,128)(2,1)S(1)}, bf16[2,32,32,128]{3,2,1,0:T(8,128)(2,1)}, u32[]{:S(2)}) copy-start(bf16[2,32,32,128]{3,2,1,0:T(8,128)(2,1)} %copy-done.5) | copy-start | bytes 1572868
  230.9 49.3 %copy-start.4 = (bf16[2,32,32,128]{3,2,1,0:T(8,128)(2,1)S(1)}, bf16[2,32,32,128]{3,2,1,0:T(8,128)(2,1)}, u32[]{:S(2)}) copy-start(bf16[2,32,32,128]{3,2,1,0:T(8,128)(2,1)} %copy-done.3) | copy-start | bytes 1572868
  300.1 15.1 %copy-start.23 = (s32[512]{0:T(512)S(1)}, s32[512]{0:T(512)}, u32[]{:S(2)}) copy-start(s32[512]{0:T(512)} %param.10) | copy-start | bytes 6148
  315.2 139.1 %copy-start.22 = (f32[2,4,128]{2,1,0:T(4,128)S(1)}, f32[2,4,128]{2,1,0:T(4,128)}, u32[]{:S(2)}) copy-start(f32[2,4,128]{2,1,0:T(4,128)} %param.12) | copy-start | bytes 12292
  (8 other events, 6.3 us)
Sparse Core Ops, SparseCore 0:
  360.9 68.7 reduce-scatter.1
